TPU v7x, 256 devices: a whole 4x4x8 slice. The times are simulated.
256 devices in a mesh: row: 16 (over x_lo, z), col: 16 (over x_hi, y, core).
Axes of the slice: x: 4 (x_hi: 2, x_lo: 2; x = x_hi * 2 + x_lo), y: 4, z: 8, core: 2. Of those that a mesh axis runs over, the one named last changes fastest.
Arguments:
- sp2_branch: int32 [3], replicated, may hold values from 0 to 1, as said below
- p0_occupancy: int32 [32, 32], replicated, may hold values from 0 to 1, as said below
- p1_occupancy: int32 [32, 32], replicated, may hold values from 0 to 1, as said below
- p0_columns: bfloat16 [73728, 512], P('col'), as said below
- p1_tiles: bfloat16 [3, 8192, 8192], P(None, 'row', 'col'), may hold values from -6 to 6, as said below
Outputs:
- p1_next: bfloat16 [3, 8192, 8192], P(None, 'row', 'col')
Inputs may be any that keep to these rules, and one draw needn't show every extreme that they name: `sp2_branch`: both values occur among the displacements. `p0_occupancy`: symmetric; every diagonal block is 1; blocks more than 8 apart around the circle of 32 blocks are 0. `p1_occupancy`: symmetric. `p0_columns`: the strips describe one symmetric matrix: a stored entry at row u and column v equals the stored entry at row v and column u; blocks more than 8 apart around the circle are zero. `p1_tiles`: each displacement's matrix is symmetric.
All inputs are finite; a program needn't handle non-finite values.
Results may differ from a plain program's by a relative error of at most 0.001.
Values may be sent and summed in bfloat16 or wider, within the bound.
No kernel may reach another device: no remote copies, remote signals or barrier semaphores. Data moves between devices by JAX's collectives and lax.ppermute only.
A program may use at most 192 MiB of HBM per device.

v0:
```python
import jax
import jax.numpy as jnp
from jax import lax
from jax.sharding import PartitionSpec as P

BLK = 256


def mask_blocks(values, occupancy):
    leading = values.shape[:-2]
    row_blocks = values.shape[-2] // BLK
    col_blocks = values.shape[-1] // BLK
    shaped = values.reshape(leading + (row_blocks, BLK, col_blocks, BLK))
    weight = occupancy.astype(values.dtype)[:, None, :, None]
    return (shaped * weight).reshape(values.shape)


def body(sp2_branch, p0_occupancy, p1_occupancy, p0_columns, p1_tiles):
    col_count = lax.axis_size("col")
    row_count = lax.axis_size("row")
    col_width = p0_columns.shape[1]
    row_height = p1_tiles.shape[1]
    col_blocks = col_width // BLK
    row_blocks = row_height // BLK
    strip_blocks = p0_columns.shape[0] // BLK
    band_half = (strip_blocks - col_blocks) // 2
    all_blocks = col_blocks * col_count
    col_span = band_half // col_blocks
    row_at = lax.axis_index("row")
    col_at = lax.axis_index("col")
    own_occ = lax.dynamic_slice(
        p1_occupancy, (row_at * row_blocks, col_at * col_blocks), (row_blocks, col_blocks)
    )
    p1_local = mask_blocks(p1_tiles, own_occ)
    tripled = jnp.concatenate([p0_occupancy, p0_occupancy, p0_occupancy], axis=0)
    strip_occ = lax.dynamic_slice(
        tripled,
        (col_at * col_blocks - band_half + all_blocks, col_at * col_blocks),
        (strip_blocks, col_blocks),
    )
    strip_local = mask_blocks(p0_columns, strip_occ)
    sign = jnp.where(col_at % 2 == 0, -1, 1)
    fetched = []
    for k in range(col_span):
        pairs = []
        for c in range(col_count):
            src = c - 1 - k if c % 2 == 0 else c + 1 + k
            pairs.append((src % col_count, c))
        fetched.append(lax.ppermute(p1_local, "col", pairs))
    swap = [(c, c ^ 1) for c in range(col_count)]
    partner_own = lax.ppermute(p1_local, "col", swap)
    partner_fetched = [lax.ppermute(fetched[j], "col", swap) for j in range(col_span - 1)]
    tiles = [(p1_local, 0)]
    tiles += [(fetched[k], sign * (k + 1)) for k in range(col_span)]
    tiles += [(partner_own, -sign)]
    tiles += [(partner_fetched[j], -sign * (j + 2)) for j in range(col_span - 1)]
    factors = []
    for _, offset in tiles:
        start = (offset + col_span) * col_width
        factors.append(lax.dynamic_slice_in_dim(strip_local, start, col_width, 0))
    summed_col = jnp.zeros(p1_local.shape, jnp.float32)
    for (tile, _), factor in zip(tiles, factors):
        summed_col = summed_col + jnp.einsum(
            "drc,ck->drk", tile, factor, preferred_element_type=jnp.float32
        )
    row_span = band_half // row_blocks
    owner_col = row_at * row_blocks // col_blocks
    mine = col_at == owner_col
    shared = lax.psum(jnp.where(mine, strip_local, jnp.zeros_like(strip_local)), "col")
    summed_row = jnp.zeros(p1_local.shape, jnp.float32)
    for e in range(-row_span, row_span + 1):
        if e == 0:
            incoming = p1_local
        else:
            incoming = lax.ppermute(
                p1_local, "row", [(r, (r - e) % row_count) for r in range(row_count)]
            )
        factor = shared[(e + row_span) * row_height : (e + row_span + 1) * row_height, :]
        summed_row = summed_row + jnp.einsum(
            "kr,dkc->drc", factor, incoming, preferred_element_type=jnp.float32
        )
    bracket = summed_col + summed_row
    squared = (sp2_branch == 1)[:, None, None]
    chosen = jnp.where(squared, bracket, 2.0 * p1_local.astype(jnp.float32) - bracket)
    return mask_blocks(chosen, own_occ).astype(jnp.bfloat16)


def solution(mesh):
    in_specs = (P(), P(), P(), P("col", None), P(None, "row", "col"))
    out_specs = P(None, "row", "col")
    return jax.shard_map(body, mesh=mesh, in_specs=in_specs, out_specs=out_specs, check_vma=False)
```

profile of v0, /device:TPU:67, one launch (start us, length us, event | category | flops | bytes accessed | tf_op | source)
XLA Modules:
  0.0 568.5 jit_solution(9399080054949832968)
XLA Ops:
  13.1 8.1 %broadcast_select_fusion = (bf16[4608,512]{1,0:T(8,128)(2,1)}, bf16[4608,512]{1,0:T(8,128)(2,1)}) fusion(pred[]{:T(512)S(6)} %eq.13, bf16[4608,512]{1,0:T(8,128)(2,1)} %param.8, bf16[4608,512]{1,0:T(8,128)(2,1)} %bitcast.86), kind=kLoop, calls=%fused_computation.1 | loop fusion | flops 4718592 | bytes 18874368 | tf_op jit(solution)/shard_map/jit(_where)/select_n | solution.py:69
  22.8 4.4 collective-permute-start.1
  32.0 7.7 %reshape.16 = bf16[18,256,2,256]{3,2,1,0:T(2,128)(2,1)} reshape(bf16[4608,512]{1,0:T(8,128)(2,1)} %param.8) | data formatting | bytes 9437184 | tf_op jit(solution)/shard_map/reshape | solution.py:13
  46.6 59.6 %collective-permute-done.1 = bf16[3,512,512]{2,1,0:T(8,128)(2,1)} collective-permute-done((bf16[3,512,512]{2,1,0:T(8,128)(2,1)S(1)}, bf16[3,512,512]{2,1,0:T(8,128)(2,1)}, u32[]{:S(2)}, u32[]{:S(2)}) %collective-permute-start.1) | collective-permute-done | bytes 1572896 | tf_op jit(solution)/shard_map/ppermute | solution.py:49
  108.0 4.6 collective-permute-done
  112.6 4.1 fusion.25
  116.7 4.1 fusion.27
  120.8 5.2 collective-permute-start.8
  126.0 4.1 fusion.19
  130.1 27.0 %collective-permute-done.3 = bf16[3,512,512]{2,1,0:T(8,128)(2,1)} collective-permute-done((bf16[3,512,512]{2,1,0:T(8,128)(2,1)S(1)}, bf16[3,512,512]{2,1,0:T(8,128)(2,1)}, u32[]{:S(2)}, u32[]{:S(2)}) %collective-permute-start.3) | collective-permute-done | bytes 1572896 | tf_op jit(solution)/shard_map/ppermute | solution.py:49
  160.9 4.1 fusion.21
  165.0 24.9 %collective-permute-start.13 = (bf16[3,512,512]{2,1,0:T(8,128)(2,1)S(1)}, bf16[3,512,512]{2,1,0:T(8,128)(2,1)}, u32[]{:S(2)}, u32[]{:S(2)}) collective-permute-start(bf16[3,512,512]{2,1,0:T(8,128)(2,1)S(1)} %broadcast_multiply_fusion), channel_id=1, source_target_pairs={{0,224},{16,240},{32,0},{48,16},{64,32},{80,48},{96,64},{112,80},{... | collective-permute-start | bytes 4718600 | tf_op jit(solution)/shard_map/ppermute | solution.py:75
  200.7 59.6 %all-reduce.2.cloned.1.call-done = bf16[4608,512]{1,0:T(8,128)(2,1)} async-done(((bf16[4608,512]{1,0:T(8,128)(2,1)}), bf16[4608,512]{1,0:T(8,128)(2,1)}) %all-reduce.2.cloned.1.call-update) | async-done | bytes 4718608 | tf_op jit(solution)/shard_map/psum | solution.py:69
  267.6 4.2 fusion.10
  271.8 21.1 %collective-permute-done.14 = bf16[3,512,512]{2,1,0:T(8,128)(2,1)} collective-permute-done((bf16[3,512,512]{2,1,0:T(8,128)(2,1)S(1)}, bf16[3,512,512]{2,1,0:T(8,128)(2,1)}, u32[]{:S(2)}, u32[]{:S(2)}) %collective-permute-start.14) | collective-permute-done | bytes 1572896 | tf_op jit(solution)/shard_map/ppermute | solution.py:75
  292.9 15.0 %collective-permute-start.9 = (bf16[3,512,512]{2,1,0:T(8,128)(2,1)S(1)}, bf16[3,512,512]{2,1,0:T(8,128)(2,1)S(1)}, u32[]{:S(2)}, u32[]{:S(2)}) collective-permute-start(bf16[3,512,512]{2,1,0:T(8,128)(2,1)S(1)} %broadcast_multiply_fusion), channel_id=1, source_target_pairs={{0,48},{16,64},{32,80},{48,96},{64,112},{80,128},{96,144},{112,160... | collective-permute-start | bytes 4718600 | tf_op jit(solution)/shard_map/ppermute | solution.py:75
  307.9 4.2 fusion.3
  312.1 56.1 %collective-permute-done.13 = bf16[3,512,512]{2,1,0:T(8,128)(2,1)} collective-permute-done((bf16[3,512,512]{2,1,0:T(8,128)(2,1)S(1)}, bf16[3,512,512]{2,1,0:T(8,128)(2,1)}, u32[]{:S(2)}, u32[]{:S(2)}) %collective-permute-start.13) | collective-permute-done | bytes 1572896 | tf_op jit(solution)/shard_map/ppermute | solution.py:75
  370.1 4.1 fusion.4
  374.2 24.0 %collective-permute-done.12 = bf16[3,512,512]{2,1,0:T(8,128)(2,1)} collective-permute-done((bf16[3,512,512]{2,1,0:T(8,128)(2,1)S(1)}, bf16[3,512,512]{2,1,0:T(8,128)(2,1)}, u32[]{:S(2)}, u32[]{:S(2)}) %collective-permute-start.12) | collective-permute-done | bytes 1572896 | tf_op jit(solution)/shard_map/ppermute | solution.py:75
  403.9 4.1 fusion.7
  410.8 26.2 %collective-permute-done.9 = bf16[3,512,512]{2,1,0:T(8,128)(2,1)S(1)} collective-permute-done((bf16[3,512,512]{2,1,0:T(8,128)(2,1)S(1)}, bf16[3,512,512]{2,1,0:T(8,128)(2,1)S(1)}, u32[]{:S(2)}, u32[]{:S(2)}) %collective-permute-start.9) | collective-permute-done | bytes 1572896 | tf_op jit(solution)/shard_map/ppermute | solution.py:75
  439.7 97.9 %collective-permute-done.15 = bf16[3,512,512]{2,1,0:T(8,128)(2,1)S(1)} collective-permute-done((bf16[3,512,512]{2,1,0:T(8,128)(2,1)S(1)}, bf16[3,512,512]{2,1,0:T(8,128)(2,1)S(1)}, u32[]{:S(2)}, u32[]{:S(2)}) %collective-permute-start.15) | collective-permute-done | bytes 1572896 | tf_op jit(solution)/shard_map/ppermute | solution.py:75
  540.2 21.4 %fusion.1 = bf16[3,512,512]{2,1,0:T(8,128)(2,1)} fusion(f32[3,512,512]{1,2,0:T(8,128)} %fusion.2, f32[3,512,512]{1,2,0:T(8,128)} %fusion.3, f32[3,512,512]{1,2,0:T(8,128)} %fusion.4, f32[3,512,512]{1,2,0:T(8,128)} %fusion.5, bf16[3,512,512]{2,1,0:T(8,128)(2,1)S(1)} %broadcast_multiply_fusion, f32[3,512,512]{1,2,0:T(8,128)} %fusion.6, ...), kind=kOutput, calls=%fused_computation.3 | convolution fusion | flops 823394304 | bytes 59768840 | tf_op jit(solution)/shard_map/drc,ck->drk/dot_general | solution.py:63
  (60 shorter events, 59.2 us)
Async XLA Ops:
  6.5 253.7 %all-reduce.2.cloned.1.call-start = ((), (), s32[]{:S(2)}) async-start(), calls=%async_computation | async-start | bytes 9437184 | tf_op jit(solution)/shard_map/psum | solution.py:69
  7.5 24.5 %copy-start.2 = (bf16[18,2]{1,0:T(8,128)(2,1)}, bf16[18,2]{1,0:T(8,128)(2,1)S(1)}, u32[]{:S(2)}) copy-start(bf16[18,2]{1,0:T(8,128)(2,1)S(1)} %copy.27) | copy-start | bytes 220
  21.1 1.4 copy-start.1
  22.8 83.5 %collective-permute-start.1 = (bf16[3,512,512]{2,1,0:T(8,128)(2,1)S(1)}, bf16[3,512,512]{2,1,0:T(8,128)(2,1)}, u32[]{:S(2)}, u32[]{:S(2)}) collective-permute-start(bf16[3,512,512]{2,1,0:T(8,128)(2,1)S(1)} %broadcast_multiply_fusion), channel_id=1, source_target_pairs={{14,0},{3,1},{0,2},{5,3},{2,4},{7,5},{4,6},{9,7},{6,8},{11,9},{8,1... | collective-permute-start | bytes 4718600 | tf_op jit(solution)/shard_map/ppermute | solution.py:49
  27.1 85.5 %collective-permute-start = (bf16[3,512,512]{2,1,0:T(8,128)(2,1)S(1)}, bf16[3,512,512]{2,1,0:T(8,128)(2,1)}, u32[]{:S(2)}, u32[]{:S(2)}) collective-permute-start(bf16[3,512,512]{2,1,0:T(8,128)(2,1)S(1)} %broadcast_multiply_fusion), channel_id=1, source_target_pairs={{15,0},{2,1},{1,2},{4,3},{3,4},{6,5},{5,6},{8,7},{7,8},{10,9},{9,1... | collective-permute-start | bytes 4718600 | tf_op jit(solution)/shard_map/ppermute | solution.py:49
  27.1 93.6 %collective-permute-start.4 = (bf16[3,512,512]{2,1,0:T(8,128)(2,1)S(1)}, bf16[3,512,512]{2,1,0:T(8,128)(2,1)}, u32[]{:S(2)}, u32[]{:S(2)}) collective-permute-start(bf16[3,512,512]{2,1,0:T(8,128)(2,1)S(1)} %broadcast_multiply_fusion), channel_id=1, source_target_pairs={{0,1},{1,0},{2,3},{3,2},{4,5},{5,4},{6,7},{7,6},{8,9},{9,8},{10,11... | collective-permute-start | bytes 4718600 | tf_op jit(solution)/shard_map/ppermute | solution.py:51
  28.0 129.1 %collective-permute-start.3 = (bf16[3,512,512]{2,1,0:T(8,128)(2,1)S(1)}, bf16[3,512,512]{2,1,0:T(8,128)(2,1)}, u32[]{:S(2)}, u32[]{:S(2)}) collective-permute-start(bf16[3,512,512]{2,1,0:T(8,128)(2,1)S(1)} %broadcast_multiply_fusion), channel_id=1, source_target_pairs={{12,0},{5,1},{14,2},{7,3},{0,4},{9,5},{2,6},{11,7},{4,8},{13,9},{6... | collective-permute-start | bytes 4718600 | tf_op jit(solution)/shard_map/ppermute | solution.py:49
  30.0 135.1 %collective-permute-start.2 = (bf16[3,512,512]{2,1,0:T(8,128)(2,1)S(1)}, bf16[3,512,512]{2,1,0:T(8,128)(2,1)}, u32[]{:S(2)}, u32[]{:S(2)}) collective-permute-start(bf16[3,512,512]{2,1,0:T(8,128)(2,1)S(1)} %broadcast_multiply_fusion), channel_id=1, source_target_pairs={{13,0},{4,1},{15,2},{6,3},{1,4},{8,5},{3,6},{10,7},{5,8},{12,9},{7... | collective-permute-start | bytes 4718600 | tf_op jit(solution)/shard_map/ppermute | solution.py:49
  32.0 7.7 %slice-start.2 = ((bf16[18,2]{1,0:T(8,128)(2,1)}), bf16[2,2]{1,0:T(2,128)(2,1)S(1)}, s32[]{:S(2)}) async-start(bf16[18,2]{1,0:T(8,128)(2,1)} %copy-done.2), calls=%async_computation.3 | async-start | bytes 1024 | tf_op jit(solution)/shard_map/dynamic_slice | solution.py:60
  42.7 74.0 %slice-start = ((s8[4718592]{0:T(1024)(128)(4,1)}), s8[524288]{0:T(1024)(128)(4,1)S(1)}, s32[]{:S(2)}) async-start(s8[4718592]{0:T(1024)(128)(4,1)} %bitcast.87), calls=%async_computation.1 | async-start | bytes 1048576
  42.8 3.8 copy-start.3
  42.8 73.9 %slice-start.1 = ((s8[4718592]{0:T(1024)(128)(4,1)}), s8[4194304]{0:T(1024)(128)(4,1)S(1)}, s32[]{:S(2)}) async-start(s8[4718592]{0:T(1024)(128)(4,1)} %bitcast.87), calls=%async_computation.2 | async-start | bytes 8388608
  106.3 87.7 %collective-permute-start.6 = (bf16[3,512,512]{2,1,0:T(8,128)(2,1)}, bf16[3,512,512]{2,1,0:T(8,128)(2,1)S(1)}, u32[]{:S(2)}, u32[]{:S(2)}) collective-permute-start(bf16[3,512,512]{2,1,0:T(8,128)(2,1)} %collective-permute-done.1), channel_id=1, source_target_pairs={{0,1},{1,0},{2,3},{3,2},{4,5},{5,4},{6,7},{7,6},{8,9},{9,8},{10,11... | collective-permute-start | bytes 4718600 | tf_op jit(solution)/shard_map/ppermute | solution.py:52
  112.6 84.0 %collective-permute-start.5 = (bf16[3,512,512]{2,1,0:T(8,128)(2,1)}, bf16[3,512,512]{2,1,0:T(8,128)(2,1)S(1)}, u32[]{:S(2)}, u32[]{:S(2)}) collective-permute-start(bf16[3,512,512]{2,1,0:T(8,128)(2,1)} %collective-permute-done), channel_id=1, source_target_pairs={{0,1},{1,0},{2,3},{3,2},{4,5},{5,4},{6,7},{7,6},{8,9},{9,8},{10,11... | collective-permute-start | bytes 4718600 | tf_op jit(solution)/shard_map/ppermute | solution.py:52
  120.8 143.3 %collective-permute-start.8 = (bf16[3,512,512]{2,1,0:T(8,128)(2,1)S(1)}, bf16[3,512,512]{2,1,0:T(8,128)(2,1)}, u32[]{:S(2)}, u32[]{:S(2)}) collective-permute-start(bf16[3,512,512]{2,1,0:T(8,128)(2,1)S(1)} %broadcast_multiply_fusion), channel_id=1, source_target_pairs={{0,64},{16,80},{32,96},{48,112},{64,128},{80,144},{96,160},{112,17... | collective-permute-start | bytes 4718600 | tf_op jit(solution)/shard_map/ppermute | solution.py:75
  157.1 135.8 %collective-permute-start.14 = (bf16[3,512,512]{2,1,0:T(8,128)(2,1)S(1)}, bf16[3,512,512]{2,1,0:T(8,128)(2,1)}, u32[]{:S(2)}, u32[]{:S(2)}) collective-permute-start(bf16[3,512,512]{2,1,0:T(8,128)(2,1)S(1)} %broadcast_multiply_fusion), channel_id=1, source_target_pairs={{0,208},{16,224},{32,240},{48,0},{64,16},{80,32},{96,48},{112,64},... | collective-permute-start | bytes 4718600 | tf_op jit(solution)/shard_map/ppermute | solution.py:75
  165.0 203.2 %collective-permute-start.13 = (bf16[3,512,512]{2,1,0:T(8,128)(2,1)S(1)}, bf16[3,512,512]{2,1,0:T(8,128)(2,1)}, u32[]{:S(2)}, u32[]{:S(2)}) collective-permute-start(bf16[3,512,512]{2,1,0:T(8,128)(2,1)S(1)} %broadcast_multiply_fusion), channel_id=1, source_target_pairs={{0,224},{16,240},{32,0},{48,16},{64,32},{80,48},{96,64},{112,80},{... | collective-permute-start | bytes 4718600 | tf_op jit(solution)/shard_map/ppermute | solution.py:75
  193.9 204.3 %collective-permute-start.12 = (bf16[3,512,512]{2,1,0:T(8,128)(2,1)S(1)}, bf16[3,512,512]{2,1,0:T(8,128)(2,1)}, u32[]{:S(2)}, u32[]{:S(2)}) collective-permute-start(bf16[3,512,512]{2,1,0:T(8,128)(2,1)S(1)} %broadcast_multiply_fusion), channel_id=1, source_target_pairs={{0,240},{16,0},{32,16},{48,32},{64,48},{80,64},{96,80},{112,96},{1... | collective-permute-start | bytes 4718600 | tf_op jit(solution)/shard_map/ppermute | solution.py:75
  196.6 207.4 %collective-permute-start.11 = (bf16[3,512,512]{2,1,0:T(8,128)(2,1)S(1)}, bf16[3,512,512]{2,1,0:T(8,128)(2,1)}, u32[]{:S(2)}, u32[]{:S(2)}) collective-permute-start(bf16[3,512,512]{2,1,0:T(8,128)(2,1)S(1)} %broadcast_multiply_fusion), channel_id=1, source_target_pairs={{0,16},{16,32},{32,48},{48,64},{64,80},{80,96},{96,112},{112,128},... | collective-permute-start | bytes 4718600 | tf_op jit(solution)/shard_map/ppermute | solution.py:75
  260.2 7.3 %copy-start = (bf16[4608,512]{1,0:T(8,128)(2,1)S(1)}, bf16[4608,512]{1,0:T(8,128)(2,1)}, u32[]{:S(2)}) copy-start(bf16[4608,512]{1,0:T(8,128)(2,1)} %all-reduce.2.cloned.1.call-done) | copy-start | bytes 14155780
  264.1 143.9 %collective-permute-start.10 = (bf16[3,512,512]{2,1,0:T(8,128)(2,1)S(1)}, bf16[3,512,512]{2,1,0:T(8,128)(2,1)S(1)}, u32[]{:S(2)}, u32[]{:S(2)}) collective-permute-start(bf16[3,512,512]{2,1,0:T(8,128)(2,1)S(1)} %broadcast_multiply_fusion), channel_id=1, source_target_pairs={{0,32},{16,48},{32,64},{48,80},{64,96},{80,112},{96,128},{112,144}... | collective-permute-start | bytes 4718600 | tf_op jit(solution)/shard_map/ppermute | solution.py:75
  292.9 144.1 %collective-permute-start.9 = (bf16[3,512,512]{2,1,0:T(8,128)(2,1)S(1)}, bf16[3,512,512]{2,1,0:T(8,128)(2,1)S(1)}, u32[]{:S(2)}, u32[]{:S(2)}) collective-permute-start(bf16[3,512,512]{2,1,0:T(8,128)(2,1)S(1)} %broadcast_multiply_fusion), channel_id=1, source_target_pairs={{0,48},{16,64},{32,80},{48,96},{64,112},{80,128},{96,144},{112,160... | collective-permute-start | bytes 4718600 | tf_op jit(solution)/shard_map/ppermute | solution.py:75
  368.2 169.4 %collective-permute-start.15 = (bf16[3,512,512]{2,1,0:T(8,128)(2,1)S(1)}, bf16[3,512,512]{2,1,0:T(8,128)(2,1)S(1)}, u32[]{:S(2)}, u32[]{:S(2)}) collective-permute-start(bf16[3,512,512]{2,1,0:T(8,128)(2,1)S(1)} %broadcast_multiply_fusion), channel_id=1, source_target_pairs={{0,192},{16,208},{32,224},{48,240},{64,0},{80,16},{96,32},{112,48}... | collective-permute-start | bytes 4718600 | tf_op jit(solution)/shard_map/ppermute | solution.py:75
  398.2 142.0 %collective-permute-start.7 = (bf16[3,512,512]{2,1,0:T(8,128)(2,1)}, bf16[3,512,512]{2,1,0:T(8,128)(2,1)}, u32[]{:S(2)}, u32[]{:S(2)}) collective-permute-start(bf16[3,512,512]{2,1,0:T(8,128)(2,1)} %collective-permute-done.2), channel_id=1, source_target_pairs={{0,1},{1,0},{2,3},{3,2},{4,5},{5,4},{6,7},{7,6},{8,9},{9,8},{10,11... | collective-permute-start | bytes 4718600 | tf_op jit(solution)/shard_map/ppermute | solution.py:52
Sparse Core Ops, SparseCore 0:
  21.3 238.8 all-reduce.1
where the time goes:
time: 569 us; the launch traced here: 568 us
  waiting for transfers between devices  376 us (66%)
  matrix products  83.4 us (15%)
  starting transfers between devices  68.4 us (12%)
  local copies, waits for them, and re-layouts  16.2 us (3%)
  between operations  13.5 us (2%)
  other arithmetic  10.8 us (2%)
    ppermute x8, waiting for transfers between devices, body(): lax.ppermute(p1_local, 'row', [(r, (r - e) % row_count) for r in range(ro...  225 us
    ppermute x4, waiting for transfers between devices, body(): fetched.append(lax.ppermute(p1_local, 'col', pairs))  91.2 us
    psum x1, waiting for transfers between devices, body(): lax.psum(jnp.where(mine, strip_local, jnp.zeros_like(strip_local)), 'col')  59.6 us
    ppermute x8, starting transfers between devices, body(): lax.ppermute(p1_local, 'row', [(r, (r - e) % row_count) for r in range(ro...  55.8 us
    dot_general x9, matrix products, body(): jnp.einsum('drc,ck->drk', tile, factor, preferred_element_type=jnp.float32)  50.8 us
    dot_general x9, matrix products, body(): jnp.einsum('kr,dkc->drc', factor, incoming, preferred_element_type=jnp.fl...  32.6 us
  transfers between devices with their start and end apart: 17, of which 9 were waited for; matrix products, arithmetic and copies ran while one was open for 13% of the time, Pallas kernels for 0%

commit v1 on v0

--- a/solution.py
+++ b/solution.py
@@ -66,7 +66,9 @@
     row_span = band_half // row_blocks
     owner_col = row_at * row_blocks // col_blocks
     mine = col_at == owner_col
-    shared = lax.psum(jnp.where(mine, strip_local, jnp.zeros_like(strip_local)), "col")
+    shared = jnp.sum(
+        lax.all_gather(jnp.where(mine, strip_local, jnp.zeros_like(strip_local)), "col"), axis=0
+    )
     summed_row = jnp.zeros(p1_local.shape, jnp.float32)
     for e in range(-row_span, row_span + 1):
         if e == 0:

time: 569 us -> 878 us (1.54)
  the two profiles are of different devices: /device:TPU:67 before, /device:TPU:13 now
where the time goes in v1:
time: 878 us
  waiting for transfers between devices  585 us (67%)
  starting transfers between devices  142 us (16%)
  matrix products  83.7 us (10%)
  other arithmetic  37.4 us (4%)
  local copies, waits for them, and re-layouts  16.4 us (2%)
  between operations  13.5 us (2%)
    all_gather x1, waiting for transfers between devices, body(): lax.all_gather(jnp.where(mine, strip_local, jnp.zeros_like(strip_local)),...  310 us
    ppermute x8, waiting for transfers between devices, body(): lax.ppermute(p1_local, 'row', [(r, (r - e) % row_count) for r in range(ro...  199 us
    ppermute x8, starting transfers between devices, body(): lax.ppermute(p1_local, 'row', [(r, (r - e) % row_count) for r in range(ro...  118 us
    ppermute x4, waiting for transfers between devices, body(): fetched.append(lax.ppermute(p1_local, 'col', pairs))  76 us
    dot_general x9, matrix products, body(): jnp.einsum('drc,ck->drk', tile, factor, preferred_element_type=jnp.float32)  51.2 us
    dot_general x9, matrix products, body(): jnp.einsum('kr,dkc->drc', factor, incoming, preferred_element_type=jnp.fl...  32.5 us
    reduce_sum x1, other arithmetic, body(): jnp.sum(lax.all_gather(jnp.where(mine, strip_local, jnp.zeros_like(strip_...  26.4 us
  transfers between devices with their start and end apart: 17, of which 4 were waited for; matrix products, arithmetic and copies ran while one was open for 12% of the time, Pallas kernels for 0%

profile of v1, /device:TPU:13, one launch (start us, length us, event | category | flops | bytes accessed | tf_op | source)
XLA Modules:
  0.0 877.7 jit_solution(6487829330307453895)
XLA Ops:
  13.0 8.1 broadcast_select_fusion
  31.7 7.9 reshape.16
  42.9 4.1 fusion.48
  46.9 58.1 %collective-permute-done.1 = bf16[3,512,512]{2,1,0:T(8,128)(2,1)} collective-permute-done((bf16[3,512,512]{2,1,0:T(8,128)(2,1)S(1)}, bf16[3,512,512]{2,1,0:T(8,128)(2,1)}, u32[]{:S(2)}, u32[]{:S(2)}) %collective-permute-start.1) | collective-permute-done | bytes 1572896 | tf_op jit(solution)/shard_map/ppermute | solution.py:49
  105.0 13.7 %collective-permute-start.5 = (bf16[3,512,512]{2,1,0:T(8,128)(2,1)}, bf16[3,512,512]{2,1,0:T(8,128)(2,1)S(1)}, u32[]{:S(2)}, u32[]{:S(2)}) collective-permute-start(bf16[3,512,512]{2,1,0:T(8,128)(2,1)} %collective-permute-done), channel_id=1, source_target_pairs={{0,1},{1,0},{2,3},{3,2},{4,5},{5,4},{6,7},{7,6},{8,9},{9,8},{10,11... | collective-permute-start | bytes 4718600 | tf_op jit(solution)/shard_map/ppermute | solution.py:52
  118.7 4.2 fusion.25
  122.9 4.1 fusion.27
  127.0 7.9 collective-permute-start.8
  134.8 4.2 fusion.19
  139.1 17.9 %collective-permute-done.3 = bf16[3,512,512]{2,1,0:T(8,128)(2,1)} collective-permute-done((bf16[3,512,512]{2,1,0:T(8,128)(2,1)S(1)}, bf16[3,512,512]{2,1,0:T(8,128)(2,1)}, u32[]{:S(2)}, u32[]{:S(2)}) %collective-permute-start.3) | collective-permute-done | bytes 1572896 | tf_op jit(solution)/shard_map/ppermute | solution.py:49
  157.0 20.7 %collective-permute-start.14 = (bf16[3,512,512]{2,1,0:T(8,128)(2,1)S(1)}, bf16[3,512,512]{2,1,0:T(8,128)(2,1)}, u32[]{:S(2)}, u32[]{:S(2)}) collective-permute-start(bf16[3,512,512]{2,1,0:T(8,128)(2,1)S(1)} %broadcast_multiply_fusion), channel_id=1, source_target_pairs={{0,208},{16,224},{32,240},{48,0},{64,16},{80,32},{96,48},{112,64},... | collective-permute-start | bytes 4718600 | tf_op jit(solution)/shard_map/ppermute | solution.py:77
  177.7 4.0 fusion.21
  182.0 4.0 fusion.23
  192.9 310.1 %all-gather.3.cloned.1.call-done = bf16[73728,512]{1,0:T(8,128)(2,1)} async-done(((bf16[4608,512]{1,0:T(8,128)(2,1)}), bf16[73728,512]{1,0:T(8,128)(2,1)}) %all-gather.3.cloned.1.call-update) | async-done | bytes 75497488 | tf_op jit(solution)/shard_map/all_gather | solution.py:70
  503.0 26.4 %reduce_sum.12 = bf16[4608,512]{1,0:T(8,128)(2,1)} reduce(bf16[16,4608,512]{2,1,0:T(8,128)(2,1)} %bitcast.8, bf16[]{:T(256)} %constant.57.clone.1), dimensions={0}, to_apply=%region_0.1 | reduce | flops 35389440 | bytes 80216064 | tf_op jit(solution)/shard_map/reduce_sum | solution.py:69
  533.3 4.1 fusion.10
  537.4 20.6 %collective-permute-start.9 = (bf16[3,512,512]{2,1,0:T(8,128)(2,1)S(1)}, bf16[3,512,512]{2,1,0:T(8,128)(2,1)S(1)}, u32[]{:S(2)}, u32[]{:S(2)}) collective-permute-start(bf16[3,512,512]{2,1,0:T(8,128)(2,1)S(1)} %broadcast_multiply_fusion), channel_id=1, source_target_pairs={{0,48},{16,64},{32,80},{48,96},{64,112},{80,128},{96,144},{112,160... | collective-permute-start | bytes 4718600 | tf_op jit(solution)/shard_map/ppermute | solution.py:77
  558.0 4.1 fusion.3
  562.1 67.0 %collective-permute-start.15 = (bf16[3,512,512]{2,1,0:T(8,128)(2,1)S(1)}, bf16[3,512,512]{2,1,0:T(8,128)(2,1)S(1)}, u32[]{:S(2)}, u32[]{:S(2)}) collective-permute-start(bf16[3,512,512]{2,1,0:T(8,128)(2,1)S(1)} %broadcast_multiply_fusion), channel_id=1, source_target_pairs={{0,192},{16,208},{32,224},{48,240},{64,0},{80,16},{96,32},{112,48}... | collective-permute-start | bytes 4718600 | tf_op jit(solution)/shard_map/ppermute | solution.py:77
  629.1 4.2 fusion.4
  634.1 4.1 fusion.5
  638.2 4.1 fusion.7
  645.1 199.0 %collective-permute-done.9 = bf16[3,512,512]{2,1,0:T(8,128)(2,1)S(1)} collective-permute-done((bf16[3,512,512]{2,1,0:T(8,128)(2,1)S(1)}, bf16[3,512,512]{2,1,0:T(8,128)(2,1)S(1)}, u32[]{:S(2)}, u32[]{:S(2)}) %collective-permute-start.9) | collective-permute-done | bytes 1572896 | tf_op jit(solution)/shard_map/ppermute | solution.py:77
  849.5 21.4 %fusion.1 = bf16[3,512,512]{2,1,0:T(8,128)(2,1)} fusion(f32[3,512,512]{1,2,0:T(8,128)} %fusion.2, f32[3,512,512]{1,2,0:T(8,128)} %fusion.3, f32[3,512,512]{1,2,0:T(8,128)} %fusion.4, f32[3,512,512]{1,2,0:T(8,128)} %fusion.5, bf16[3,512,512]{2,1,0:T(8,128)(2,1)S(1)} %broadcast_multiply_fusion, f32[3,512,512]{1,2,0:T(8,128)} %fusion.6, ...), kind=kOutput, calls=%fused_computation.3 | convolution fusion | flops 823394304 | bytes 59768840 | tf_op jit(solution)/shard_map/drc,ck->drk/dot_general | solution.py:63
  (61 shorter events, 40.3 us)
Async XLA Ops:
  6.5 496.5 %all-gather.3.cloned.1.call-start = ((), (), s32[]{:S(2)}) async-start(), calls=%async_computation | async-start | bytes 80216064 | tf_op jit(solution)/shard_map/all_gather | solution.py:70
  7.5 24.1 %copy-start.2 = (bf16[18,2]{1,0:T(8,128)(2,1)}, bf16[18,2]{1,0:T(8,128)(2,1)S(1)}, u32[]{:S(2)}) copy-start(bf16[18,2]{1,0:T(8,128)(2,1)S(1)} %copy.27) | copy-start | bytes 220
  21.1 1.4 copy-start.1
  22.7 82.3 %collective-permute-start.1 = (bf16[3,512,512]{2,1,0:T(8,128)(2,1)S(1)}, bf16[3,512,512]{2,1,0:T(8,128)(2,1)}, u32[]{:S(2)}, u32[]{:S(2)}) collective-permute-start(bf16[3,512,512]{2,1,0:T(8,128)(2,1)S(1)} %broadcast_multiply_fusion), channel_id=1, source_target_pairs={{14,0},{3,1},{0,2},{5,3},{2,4},{7,5},{4,6},{9,7},{6,8},{11,9},{8,1... | collective-permute-start | bytes 4718600 | tf_op jit(solution)/shard_map/ppermute | solution.py:49
  23.0 82.1 %collective-permute-start = (bf16[3,512,512]{2,1,0:T(8,128)(2,1)S(1)}, bf16[3,512,512]{2,1,0:T(8,128)(2,1)}, u32[]{:S(2)}, u32[]{:S(2)}) collective-permute-start(bf16[3,512,512]{2,1,0:T(8,128)(2,1)S(1)} %broadcast_multiply_fusion), channel_id=1, source_target_pairs={{15,0},{2,1},{1,2},{4,3},{3,4},{6,5},{5,6},{8,7},{7,8},{10,9},{9,1... | collective-permute-start | bytes 4718600 | tf_op jit(solution)/shard_map/ppermute | solution.py:49
  25.9 101.0 %collective-permute-start.4 = (bf16[3,512,512]{2,1,0:T(8,128)(2,1)S(1)}, bf16[3,512,512]{2,1,0:T(8,128)(2,1)}, u32[]{:S(2)}, u32[]{:S(2)}) collective-permute-start(bf16[3,512,512]{2,1,0:T(8,128)(2,1)S(1)} %broadcast_multiply_fusion), channel_id=1, source_target_pairs={{0,1},{1,0},{2,3},{3,2},{4,5},{5,4},{6,7},{7,6},{8,9},{9,8},{10,11... | collective-permute-start | bytes 4718600 | tf_op jit(solution)/shard_map/ppermute | solution.py:51
  26.1 130.9 %collective-permute-start.3 = (bf16[3,512,512]{2,1,0:T(8,128)(2,1)S(1)}, bf16[3,512,512]{2,1,0:T(8,128)(2,1)}, u32[]{:S(2)}, u32[]{:S(2)}) collective-permute-start(bf16[3,512,512]{2,1,0:T(8,128)(2,1)S(1)} %broadcast_multiply_fusion), channel_id=1, source_target_pairs={{12,0},{5,1},{14,2},{7,3},{0,4},{9,5},{2,6},{11,7},{4,8},{13,9},{6... | collective-permute-start | bytes 4718600 | tf_op jit(solution)/shard_map/ppermute | solution.py:49
  29.3 152.4 %collective-permute-start.2 = (bf16[3,512,512]{2,1,0:T(8,128)(2,1)S(1)}, bf16[3,512,512]{2,1,0:T(8,128)(2,1)}, u32[]{:S(2)}, u32[]{:S(2)}) collective-permute-start(bf16[3,512,512]{2,1,0:T(8,128)(2,1)S(1)} %broadcast_multiply_fusion), channel_id=1, source_target_pairs={{13,0},{4,1},{15,2},{6,3},{1,4},{8,5},{3,6},{10,7},{5,8},{12,9},{7... | collective-permute-start | bytes 4718600 | tf_op jit(solution)/shard_map/ppermute | solution.py:49
  31.7 7.9 slice-start.2
  42.7 80.1 %slice-start = ((s8[4718592]{0:T(1024)(128)(4,1)}), s8[524288]{0:T(1024)(128)(4,1)S(1)}, s32[]{:S(2)}) async-start(s8[4718592]{0:T(1024)(128)(4,1)} %bitcast.88), calls=%async_computation.1 | async-start | bytes 1048576
  42.8 4.1 copy-start.3
  42.9 80.0 %slice-start.1 = ((s8[4718592]{0:T(1024)(128)(4,1)}), s8[4194304]{0:T(1024)(128)(4,1)S(1)}, s32[]{:S(2)}) async-start(s8[4718592]{0:T(1024)(128)(4,1)} %bitcast.88), calls=%async_computation.2 | async-start | bytes 8388608
  105.0 81.0 %collective-permute-start.6 = (bf16[3,512,512]{2,1,0:T(8,128)(2,1)}, bf16[3,512,512]{2,1,0:T(8,128)(2,1)S(1)}, u32[]{:S(2)}, u32[]{:S(2)}) collective-permute-start(bf16[3,512,512]{2,1,0:T(8,128)(2,1)} %collective-permute-done.1), channel_id=1, source_target_pairs={{0,1},{1,0},{2,3},{3,2},{4,5},{5,4},{6,7},{7,6},{8,9},{9,8},{10,11... | collective-permute-start | bytes 4718600 | tf_op jit(solution)/shard_map/ppermute | solution.py:52
  105.0 84.1 %collective-permute-start.5 = (bf16[3,512,512]{2,1,0:T(8,128)(2,1)}, bf16[3,512,512]{2,1,0:T(8,128)(2,1)S(1)}, u32[]{:S(2)}, u32[]{:S(2)}) collective-permute-start(bf16[3,512,512]{2,1,0:T(8,128)(2,1)} %collective-permute-done), channel_id=1, source_target_pairs={{0,1},{1,0},{2,3},{3,2},{4,5},{5,4},{6,7},{7,6},{8,9},{9,8},{10,11... | collective-permute-start | bytes 4718600 | tf_op jit(solution)/shard_map/ppermute | solution.py:52
  127.0 406.3 %collective-permute-start.8 = (bf16[3,512,512]{2,1,0:T(8,128)(2,1)S(1)}, bf16[3,512,512]{2,1,0:T(8,128)(2,1)}, u32[]{:S(2)}, u32[]{:S(2)}) collective-permute-start(bf16[3,512,512]{2,1,0:T(8,128)(2,1)S(1)} %broadcast_multiply_fusion), channel_id=1, source_target_pairs={{0,64},{16,80},{32,96},{48,112},{64,128},{80,144},{96,160},{112,17... | collective-permute-start | bytes 4718600 | tf_op jit(solution)/shard_map/ppermute | solution.py:77
  157.0 380.4 %collective-permute-start.14 = (bf16[3,512,512]{2,1,0:T(8,128)(2,1)S(1)}, bf16[3,512,512]{2,1,0:T(8,128)(2,1)}, u32[]{:S(2)}, u32[]{:S(2)}) collective-permute-start(bf16[3,512,512]{2,1,0:T(8,128)(2,1)S(1)} %broadcast_multiply_fusion), channel_id=1, source_target_pairs={{0,208},{16,224},{32,240},{48,0},{64,16},{80,32},{96,48},{112,64},... | collective-permute-start | bytes 4718600 | tf_op jit(solution)/shard_map/ppermute | solution.py:77
  181.7 380.4 %collective-permute-start.13 = (bf16[3,512,512]{2,1,0:T(8,128)(2,1)S(1)}, bf16[3,512,512]{2,1,0:T(8,128)(2,1)}, u32[]{:S(2)}, u32[]{:S(2)}) collective-permute-start(bf16[3,512,512]{2,1,0:T(8,128)(2,1)S(1)} %broadcast_multiply_fusion), channel_id=1, source_target_pairs={{0,224},{16,240},{32,0},{48,16},{64,32},{80,48},{96,64},{112,80},{... | collective-permute-start | bytes 4718600 | tf_op jit(solution)/shard_map/ppermute | solution.py:77
  186.0 447.3 %collective-permute-start.12 = (bf16[3,512,512]{2,1,0:T(8,128)(2,1)S(1)}, bf16[3,512,512]{2,1,0:T(8,128)(2,1)}, u32[]{:S(2)}, u32[]{:S(2)}) collective-permute-start(bf16[3,512,512]{2,1,0:T(8,128)(2,1)S(1)} %broadcast_multiply_fusion), channel_id=1, source_target_pairs={{0,240},{16,0},{32,16},{48,32},{64,48},{80,64},{96,80},{112,96},{1... | collective-permute-start | bytes 4718600 | tf_op jit(solution)/shard_map/ppermute | solution.py:77
  189.1 449.1 %collective-permute-start.11 = (bf16[3,512,512]{2,1,0:T(8,128)(2,1)S(1)}, bf16[3,512,512]{2,1,0:T(8,128)(2,1)}, u32[]{:S(2)}, u32[]{:S(2)}) collective-permute-start(bf16[3,512,512]{2,1,0:T(8,128)(2,1)S(1)} %broadcast_multiply_fusion), channel_id=1, source_target_pairs={{0,16},{16,32},{32,48},{48,64},{64,80},{80,96},{96,112},{112,128},... | collective-permute-start | bytes 4718600 | tf_op jit(solution)/shard_map/ppermute | solution.py:77
  529.4 3.9 copy-start
  533.3 109.0 %collective-permute-start.10 = (bf16[3,512,512]{2,1,0:T(8,128)(2,1)S(1)}, bf16[3,512,512]{2,1,0:T(8,128)(2,1)S(1)}, u32[]{:S(2)}, u32[]{:S(2)}) collective-permute-start(bf16[3,512,512]{2,1,0:T(8,128)(2,1)S(1)} %broadcast_multiply_fusion), channel_id=1, source_target_pairs={{0,32},{16,48},{32,64},{48,80},{64,96},{80,112},{96,128},{112,144}... | collective-permute-start | bytes 4718600 | tf_op jit(solution)/shard_map/ppermute | solution.py:77
  537.4 306.7 %collective-permute-start.9 = (bf16[3,512,512]{2,1,0:T(8,128)(2,1)S(1)}, bf16[3,512,512]{2,1,0:T(8,128)(2,1)S(1)}, u32[]{:S(2)}, u32[]{:S(2)}) collective-permute-start(bf16[3,512,512]{2,1,0:T(8,128)(2,1)S(1)} %broadcast_multiply_fusion), channel_id=1, source_target_pairs={{0,48},{16,64},{32,80},{48,96},{64,112},{80,128},{96,144},{112,160... | collective-permute-start | bytes 4718600 | tf_op jit(solution)/shard_map/ppermute | solution.py:77
  562.1 284.7 %collective-permute-start.15 = (bf16[3,512,512]{2,1,0:T(8,128)(2,1)S(1)}, bf16[3,512,512]{2,1,0:T(8,128)(2,1)S(1)}, u32[]{:S(2)}, u32[]{:S(2)}) collective-permute-start(bf16[3,512,512]{2,1,0:T(8,128)(2,1)S(1)} %broadcast_multiply_fusion), channel_id=1, source_target_pairs={{0,192},{16,208},{32,224},{48,240},{64,0},{80,16},{96,32},{112,48}... | collective-permute-start | bytes 4718600 | tf_op jit(solution)/shard_map/ppermute | solution.py:77
  633.3 216.2 %collective-permute-start.7 = (bf16[3,512,512]{2,1,0:T(8,128)(2,1)}, bf16[3,512,512]{2,1,0:T(8,128)(2,1)}, u32[]{:S(2)}, u32[]{:S(2)}) collective-permute-start(bf16[3,512,512]{2,1,0:T(8,128)(2,1)} %collective-permute-done.2), channel_id=1, source_target_pairs={{0,1},{1,0},{2,3},{3,2},{4,5},{5,4},{6,7},{7,6},{8,9},{9,8},{10,11... | collective-permute-start | bytes 4718600 | tf_op jit(solution)/shard_map/ppermute | solution.py:52
Sparse Core Ops, SparseCore 0:
  21.3 481.7 all-gather.2
